TPU v7x, 32 devices: a whole 2x2x4 slice. The times are simulated.
32 devices in a mesh: row: 8 (over z, x), col: 4 (over y, core).
Axes of the slice: x: 2, y: 2, z: 4, core: 2. Of those that a mesh axis runs over, the one named last changes fastest.
Arguments:
- amplitudes: bfloat16 [3072, 65536], P('row', 'col'), may hold values from -6 to 6
- integrals: bfloat16 [65536, 1024], P('col', 'row'), may hold values from -0.09375 to 0.09375
- pair_label: int32 [24], P('row'), may hold values from 0 to 7
- orbital_irrep: int32 [256], replicated, may hold values from 0 to 7
- column_label: int32 [8], replicated, may hold values from 0 to 7
Outputs:
- ladder: bfloat16 [1024, 3072], P('col', 'row')
Inputs may be any that keep to these rules, and one draw needn't show every extreme that they name: `orbital_irrep`: irrep labels of the window's virtual orbitals.
All inputs are finite; a program needn't handle non-finite values.
Results may differ from a plain program's by a relative error of at most 0.001.
Values may be sent and summed in bfloat16 or wider, within the bound.
No kernel may reach another device: no remote copies, remote signals or barrier semaphores. Data moves between devices by JAX's collectives and lax.ppermute only.
A program may use at most 128 MiB of HBM per device.

v0:
```python
import jax
import jax.numpy as jnp
from jax import lax
from jax.sharding import PartitionSpec as P

PAIR_BLOCK = 128


def body(amplitudes, integrals, pair_label, orbital_irrep, column_label):
    pair_rows, cd_count = amplitudes.shape
    orb_width = orbital_irrep.shape[0]
    c_count = cd_count // orb_width
    c_start = lax.axis_index("col") * c_count
    c_irrep = lax.dynamic_slice_in_dim(orbital_irrep, c_start, c_count)
    cd_label = jnp.bitwise_xor(c_irrep[:, None], orbital_irrep[None, :]).reshape(cd_count)
    row_label = jnp.repeat(pair_label, pair_rows // pair_label.shape[0])
    amp_keep = row_label[:, None] == cd_label[None, :]
    ab_label = jnp.repeat(column_label, PAIR_BLOCK)
    slab_keep = cd_label[:, None] == ab_label[None, :]
    amp_kept = jnp.where(amp_keep, amplitudes, jnp.zeros_like(amplitudes))
    ab_count = integrals.shape[1]
    int_cube = integrals.reshape(c_count, orb_width, ab_count)
    swapped = lax.all_to_all(int_cube, "col", split_axis=1, concat_axis=0, tiled=True)
    mirrored = jnp.transpose(swapped, (1, 0, 2)).reshape(cd_count, ab_count)
    int_slab, mirror_slab = (
        lax.all_gather(integrals, "row", axis=1, tiled=True),
        lax.all_gather(mirrored, "row", axis=1, tiled=True),
    )
    int_kept = jnp.where(slab_keep, int_slab, jnp.zeros_like(int_slab))
    mirror_kept = jnp.where(slab_keep, mirror_slab, jnp.zeros_like(mirror_slab))
    direct = jnp.einsum("ka,pk->ap", int_kept, amp_kept, preferred_element_type=jnp.float32)
    crossed = jnp.einsum("ka,pk->ap", mirror_kept, amp_kept, preferred_element_type=jnp.float32)
    summed = lax.psum_scatter(direct - crossed, "col", scatter_dimension=0, tiled=True)
    return summed.astype(jnp.bfloat16)


def solution(mesh):
    placed = (P("row", "col"), P("col", "row"), P("row"), P(), P())
    return jax.shard_map(
        body, mesh=mesh, in_specs=placed, out_specs=P("col", "row"), check_vma=False
    )
```

profile of v0, /device:TPU:0, one launch (start us, length us, event | category | flops | bytes accessed | tf_op | source)
XLA Modules:
  0.0 1354.9 jit_solution(896784742545501466)
XLA Ops:
  6.5 0.0 copy-start
  6.5 0.0 all-gather.3.cloned.1.call-start
  6.5 0.7 all-gather.3.cloned.1.call-update
  7.3 0.0 all-gather.5.cloned.1.call-start
  7.3 4.9 copy.8
  12.2 52.2 %all_to_all.18 = bf16[64,256,128]{2,0,1:T(8,128)(2,1)S(1)} all-to-all(bf16[64,256,128]{2,0,1:T(8,128)(2,1)S(1)} %copy.8), channel_id=1, replica_groups=mesh['row'=8,'col'=4] {'col'}, dimensions={1} | all-to-all | bytes 8388608 | tf_op jit(solution)/shard_map/all_to_all | solution.py:23
  64.4 0.0 copy-start.2
  64.4 0.0 copy-start.3
  64.4 2.7 copy.10
  67.1 4.7 copy.11
  71.8 0.0 all-gather.5.cloned.1.call-update
  71.8 0.2 reduce-scatter.2.cloned.1.call-start
  72.1 0.0 copy-done.2
  72.1 0.1 dynamic_slice.3
  72.1 0.1 xor_bitcast_fusion
  72.3 0.0 copy-done.3
  72.3 0.1 broadcast_bitcast_fusion.1
  72.3 0.0 copy-done
  72.4 0.1 broadcast_bitcast_fusion
  72.4 578.2 %all-gather.3.cloned.1.call-done = bf16[16384,1024]{1,0:T(8,128)(2,1)} async-done(((bf16[16384,128]{1,0:T(8,128)(2,1)}), bf16[16384,1024]{1,0:T(8,128)(2,1)}) %all-gather.3.cloned.1.call-update) | async-done | bytes 33554448 | tf_op jit(solution)/shard_map/all_gather | solution.py:26
  650.6 25.8 %fusion = f32[1024,384]{1,0:T(8,128)S(1)} fusion(bf16[16384,1024]{1,0:T(8,128)(2,1)} %all-gather.3.cloned.1.call-done, s32[1024]{0:T(1024)S(1)} %broadcast_bitcast_fusion, s32[16384]{0:T(1024)S(1)} %bitcast.19, bf16[384,16384]{1,0:T(8,128)(2,1)} %param.5, s32[384]{0:T(512)S(1)} %broadcast_bitcast_fusion.1), kind=kOutput, calls=%fused_computation.2 | convolution fusion | flops 12931039232 | bytes 47781376 | tf_op jit(solution)/shard_map/ka,pk->ap/dot_general | solution.py:31
  676.4 614.8 %all-gather.5.cloned.1.call-done = bf16[16384,1024]{1,0:T(8,128)(2,1)} async-done(((bf16[16384,128]{1,0:T(8,128)(2,1)}), bf16[16384,1024]{1,0:T(8,128)(2,1)}) %all-gather.5.cloned.1.call-update) | async-done | bytes 33554448 | tf_op jit(solution)/shard_map/all_gather | solution.py:27
  1291.2 0.0 copy-start.1
  1291.2 27.1 %fusion.8 = f32[1024,384]{1,0:T(8,128)} fusion(f32[1024,384]{1,0:T(8,128)S(1)} %fusion, bf16[384,16384]{1,0:T(8,128)(2,1)} %param.5, s32[16384]{0:T(1024)S(1)} %bitcast.20, s32[384]{0:T(512)S(1)} %broadcast_bitcast_fusion.1, bf16[16384,1024]{1,0:T(8,128)(2,1)} %all-gather.5.cloned.1.call-done, s32[1024]{0:T(1024)S(1)} %broadcast_bitcast_fusion), kind=kOutput, calls=%fused_computation.11 | convolution fusion | flops 12931432448 | bytes 49354240 | tf_op jit(solution)/shard_map/ka,pk->ap/dot_general | solution.py:32
  1318.3 0.0 reduce-scatter.2.cloned.1.call-update
  1318.3 28.4 %reduce-scatter.2.cloned.1.call-done = f32[256,384]{1,0:T(8,128)} async-done(((f32[1024,384]{1,0:T(8,128)}), f32[256,384]{1,0:T(8,128)}) %reduce-scatter.2.cloned.1.call-update) | async-done | bytes 393232 | tf_op jit(solution)/shard_map/reduce_scatter | solution.py:33
  1346.7 1.7 convert_element_type.3
  1348.4 0.0 copy-done.1
  (1 shorter events, 0.0 us)
Async XLA Ops:
  6.5 65.8 %copy-start = (s32[8]{0:T(128)S(1)}, s32[8]{0:T(128)}, u32[]{:S(2)}) copy-start(s32[8]{0:T(128)} %param.9) | copy-start | bytes 100
  6.5 644.1 %all-gather.3.cloned.1.call-start = ((), (), s32[]{:S(2)}) async-start(), calls=%async_computation.2 | async-start | bytes 37748736 | tf_op jit(solution)/shard_map/all_gather | solution.py:26
  7.3 1283.9 %all-gather.5.cloned.1.call-start = ((), (), s32[]{:S(2)}) async-start(), calls=%async_computation.3 | async-start | bytes 37748736 | tf_op jit(solution)/shard_map/all_gather | solution.py:27
  64.4 7.7 copy-start.2
  64.4 7.9 copy-start.3
  71.8 1274.9 %reduce-scatter.2.cloned.1.call-start = ((), (), s32[]{:S(2)}) async-start(), calls=%async_computation.4 | async-start | bytes 1966080 | tf_op jit(solution)/shard_map/reduce_scatter | solution.py:33
  1291.2 57.2 %copy-start.1 = (s32[8]{0:T(128)S(1)}, s32[8]{0:T(128)}, u32[]{:S(2)}) copy-start(s32[8]{0:T(128)} %param.9) | copy-start | bytes 100
Sparse Core Ops, SparseCore 0:
  8.8 641.7 all-gather.2
  652.1 639.0 all-gather.4
  1318.4 28.1 reduce-scatter.1
where the time goes:
time: 1360 us; the launch traced here: 1350 us
  waiting for transfers between devices  1220 us (90%)
  matrix products  52.9 us (4%)
  blocking collectives  52.2 us (4%)
    all_gather x1, waiting for transfers between devices, body(): lax.all_gather(mirrored, 'row', axis=1, tiled=True)  615 us
    all_gather x1, waiting for transfers between devices, body(): lax.all_gather(integrals, 'row', axis=1, tiled=True)  578 us
    all_to_all x1, blocking collectives, body(): lax.all_to_all(int_cube, 'col', split_axis=1, concat_axis=0, tiled=True)  52.2 us
    reduce_scatter x1, waiting for transfers between devices, body(): lax.psum_scatter(direct - crossed, 'col', scatter_dimension=0, tiled=True)  28.4 us
  transfers between devices with their start and end apart: 3, of which 3 were waited for; matrix products, arithmetic and copies ran while one was open for 3% of the time, Pallas kernels for 0%

commit v1 on v0

v1 whole, which is shorter than its diff:
```python
import jax
import jax.numpy as jnp
from jax import lax
from jax.sharding import PartitionSpec as P

PAIR_BLOCK = 128
IRREPS = 8
TIERS = (4, 5, 8)


def make_body(n_row, n_col):
    def body(amplitudes, integrals, pair_label, orbital_irrep, column_label):
        pair_rows, cd_count = amplitudes.shape
        orb_width = orbital_irrep.shape[0]
        c_count = cd_count // orb_width
        ab_count = integrals.shape[1]
        col_i = lax.axis_index("col")
        row_i = lax.axis_index("row")
        c_irrep = lax.dynamic_slice_in_dim(orbital_irrep, col_i * c_count, c_count)
        cd_label = jnp.bitwise_xor(c_irrep[:, None], orbital_irrep[None, :]).reshape(cd_count)
        row_label = jnp.repeat(pair_label, pair_rows // pair_label.shape[0])
        int_cube = integrals.reshape(c_count, orb_width, ab_count)
        swapped = lax.all_to_all(int_cube, "col", split_axis=1, concat_axis=0, tiled=True)
        mirrored = jnp.transpose(swapped, (1, 0, 2)).reshape(cd_count, ab_count)

        def dense(_):
            ab_label = jnp.repeat(column_label, PAIR_BLOCK)
            amp_keep = row_label[:, None] == cd_label[None, :]
            slab_keep = cd_label[:, None] == ab_label[None, :]
            amp_kept = jnp.where(amp_keep, amplitudes, jnp.zeros_like(amplitudes))
            int_slab = lax.all_gather(integrals, "row", axis=1, tiled=True)
            mirror_slab = lax.all_gather(mirrored, "row", axis=1, tiled=True)
            int_kept = jnp.where(slab_keep, int_slab, jnp.zeros_like(int_slab))
            mirror_kept = jnp.where(slab_keep, mirror_slab, jnp.zeros_like(mirror_slab))
            direct = jnp.einsum("ka,pk->ap", int_kept, amp_kept, preferred_element_type=jnp.float32)
            crossed = jnp.einsum("ka,pk->ap", mirror_kept, amp_kept, preferred_element_type=jnp.float32)
            return direct - crossed

        single = ab_count <= PAIR_BLOCK and PAIR_BLOCK % ab_count == 0
        if not single:
            partial = dense(None)
        else:
            block_label = column_label[(jnp.arange(n_row) * ab_count) // PAIR_BLOCK]
            irreps = jnp.arange(IRREPS, dtype=orbital_irrep.dtype)
            per_irrep = jnp.sum(orbital_irrep[:, None] == irreps[None, :], axis=0)
            per_orb = per_irrep[jnp.bitwise_xor(orbital_irrep[:, None], irreps[None, :])]
            per_col = per_orb.reshape(n_col, c_count, IRREPS).sum(axis=1)
            kept = per_col[:, block_label]
            largest = jnp.max(kept)
            own_counts = per_col[col_i][block_label]
            caps = [t * cd_count // 16 for t in TIERS]
            tier = sum((largest > cap).astype(jnp.int32) for cap in caps)

            def compact(cap):
                def run(_):
                    masks = cd_label[None, :] == block_label[:, None]
                    pos = jnp.cumsum(masks.astype(jnp.int32), axis=1) - 1
                    target = jnp.where(masks, pos, cap)
                    src = jnp.broadcast_to(jnp.arange(cd_count, dtype=jnp.int32), masks.shape)
                    lane = jnp.broadcast_to(jnp.arange(n_row, dtype=jnp.int32)[:, None], masks.shape)
                    idx = jnp.zeros((n_row, cap), jnp.int32).at[lane, target].set(src, mode="drop")
                    valid = jnp.arange(cap)[None, :] < own_counts[:, None]
                    own_idx = idx[row_i]
                    own_valid = valid[row_i][:, None]
                    sent = jnp.concatenate(
                        [jnp.take(integrals, own_idx, axis=0), jnp.take(mirrored, own_idx, axis=0)], axis=1
                    )
                    sent = jnp.where(own_valid, sent, jnp.zeros_like(sent))
                    got = lax.all_gather(sent, "row", axis=0, tiled=False)
                    amp_rows = jnp.take(amplitudes.T, idx, axis=0)
                    prod = jnp.einsum("imq,imp->iqp", got, amp_rows, preferred_element_type=jnp.float32)
                    diff = prod[:, :ab_count] - prod[:, ab_count:]
                    keep = row_label[None, :] == block_label[:, None]
                    diff = jnp.where(keep[:, None, :], diff, jnp.zeros_like(diff))
                    return diff.reshape(n_row * ab_count, pair_rows)

                return run

            branches = [compact(cap) for cap in caps] + [dense]
            partial = lax.switch(tier, branches, None)
        summed = lax.psum_scatter(partial, "col", scatter_dimension=0, tiled=True)
        return summed.astype(jnp.bfloat16)

    return body


def solution(mesh):
    placed = (P("row", "col"), P("col", "row"), P("row"), P(), P())
    return jax.shard_map(
        make_body(mesh.shape["row"], mesh.shape["col"]),
        mesh=mesh,
        in_specs=placed,
        out_specs=P("col", "row"),
        check_vma=False,
    )
```

time: 1360 us -> 906 us (0.67)
  waiting for transfers between devices: 1220 us -> 146 us
  local copies, waits for them, and re-layouts: 12.5 us -> 678 us
  blocking collectives: 52.2 us -> 0 us
  matrix products: 52.9 us -> 19.3 us
  loops' own time: 0 us -> 17.7 us
    all_gather x2 -> x1, waiting for transfers between devices: 1190 us -> 78.8 us  [run(): got = lax.all_gather(sent, 'row', axis=0, tiled=False)]
    cond x0 -> x10, local copies, waits for them, and re-layouts: none -> 479 us
    gather x0 -> x7, local copies, waits for them, and re-layouts: none -> 163 us  [the longest x1 133 us: run(): amp_rows = jnp.take(amplitudes.T, idx, axis=0)]
    all_to_all x1 -> x0, blocking collectives: 52.2 us -> none  [body(): lax.all_to_all(int_cube, 'col', split_axis=1, concat_axis=0, tiled=True)]
    all_to_all x0 -> x1, waiting for transfers between devices: none -> 38.9 us  [body(): lax.all_to_all(int_cube, 'col', split_axis=1, concat_axis=0, tiled=True)]
    dot_general x2 -> x1, matrix products: 52.9 us -> 19.3 us  [run(): jnp.einsum('imq,imp->iqp', got, amp_rows, preferred_element_type=jnp.floa...]
    another operation x0 -> x1, loops' own time: none -> 17.7 us  [body(): partial = lax.switch(tier, branches, None)]
    another operation x0 -> x4, local copies, waits for them, and re-layouts: none -> 17 us
  transfers between devices with their start and end apart: 3 -> 3, of which waited for: 3 -> 3; matrix products, arithmetic and copies ran while one was open for 3% -> 18% of each run, Pallas kernels for 0% -> 0%
where the time goes in v1:
time: 906 us; the launch traced here: 899 us
  local copies, waits for them, and re-layouts  678 us (75%)
  waiting for transfers between devices  146 us (16%)
  matrix products  19.3 us (2%)
  loops' own time  17.7 us (2%)
  between operations  17.4 us (2%)
  other arithmetic  15.1 us (2%)
    cond x10, local copies, waits for them, and re-layouts  479 us
    gather x1, local copies, waits for them, and re-layouts, run(): amp_rows = jnp.take(amplitudes.T, idx, axis=0)  133 us
    all_gather x1, waiting for transfers between devices, run(): got = lax.all_gather(sent, 'row', axis=0, tiled=False)  78.8 us
    all_to_all x1, waiting for transfers between devices, body(): lax.all_to_all(int_cube, 'col', split_axis=1, concat_axis=0, tiled=True)  38.9 us
    reduce_scatter x1, waiting for transfers between devices, body(): summed = lax.psum_scatter(partial, 'col', scatter_dimension=0, tiled=True)  28.2 us
    dot_general x1, matrix products, run(): jnp.einsum('imq,imp->iqp', got, amp_rows, preferred_element_type=jnp.floa...  19.3 us
  transfers between devices with their start and end apart: 3, of which 3 were waited for; matrix products, arithmetic and copies ran while one was open for 18% of the time, Pallas kernels for 0%

profile of v1, /device:TPU:0, one launch (start us, length us, event | category | flops | bytes accessed | tf_op | source)
XLA Modules:
  0.0 898.6 jit_solution(17592914409914368684)
XLA Ops:
  7.4 6.9 copy.101
  14.2 0.0 copy-start.9
  14.2 0.0 copy-start
  14.2 5.0 all-to-all-start
  19.2 0.0 copy-done.9
  19.2 0.1 dynamic_slice.40
  19.3 0.1 convert_reduce_fusion
  19.4 0.7 fusion.66
  20.1 4.9 bitcast_select_fusion
  25.0 0.1 reshape.756
  25.1 0.2 reduce_sum.19
  25.3 0.0 copy-done
  25.3 0.6 gather_fusion.12
  26.0 0.6 gather_fusion.13
  26.5 0.6 reduce_max.9
  29.1 0.1 broadcast_xor_fusion
  29.2 38.9 %all-to-all-done = bf16[64,256,128]{2,0,1:T(8,128)(2,1)} async-done(((bf16[64,256,128]{2,0,1:T(8,128)(2,1)}), bf16[64,256,128]{2,0,1:T(8,128)(2,1)}, u32[]{:S(2)}, u32[]{:S(2)}) %all-to-all-start) | async-done | bytes 4194336 | tf_op jit(solution)/shard_map/all_to_all | solution.py:23
  68.1 4.9 copy.103
  73.0 0.0 copy-start.16
  73.0 4.7 copy.104
  77.7 0.0 copy-done.16
  77.7 0.1 broadcast_in_dim.179
  77.7 781.9 %conditional.1 = (f32[1024,384]{1,0:T(8,128)S(1)}) conditional(s32[]{:T(128)} %clamp.3, (s32[3,128]{1,0:T(4,128)S(1)}, s32[8]{0:T(128)S(1)}, s32[]{:T(128)}, s32[4,8]{0,1:T(8,128)S(1)}, s32[8,1]{0,1:T(1,128)S(1)}, /*index=5*/s32[]{:T(128)}, s32[64,256]{1,0:T(8,128)S(1)}, bf16[16384,128]{1,0:T(8,128)(2,1)}, ...), branch_computations={%region_3.8_spmd, %region_7.13_spmd, %region_11.18_spmd, %region_1... | conditional | flops 25862471680 | bytes 371643616 | solution.py:80
  77.7 0.0 copy-start.13
  77.7 0.0 copy-start.10
  77.7 0.5 all-gather.6.cloned.1.call-start
  78.4 0.1 copy.92
  78.5 0.2 fusion.16
  78.7 0.3 reduce-window.13
  79.0 0.2 copy.93
  79.3 0.1 sub.19
  79.4 0.2 compare_select_fusion.11
  79.6 0.0 copy-done.13
  79.6 0.3 and_reduce_fusion
  79.9 0.0 copy-done.10
  79.9 0.1 multiply_reduce_fusion
  80.0 0.1 select_bitcast_fusion.2
  80.1 0.1 copy.117
  80.2 0.1 copy.118
  80.3 478.4 %scatter_custom_fusion = s32[32768]{0:T(1024)S(1)} fusion(s32[131072]{0:T(1024)S(1)} %bitcast.141, s32[131072]{0:T(1024)S(1)} %bitcast.144, s32[]{:T(128)} %constant.74.clone), kind=kCustom, calls=%fused_computation.57 | custom fusion | bytes 131076 | tf_op jit(solution)/shard_map/cond
  558.8 0.1 copy.105
  558.9 0.6 gather_fusion
  559.6 0.6 dynamic-slice
  560.1 0.7 compare_reduce_fusion
  560.9 13.8 %gather_fusion.3 = bf16[4096,128]{1,0:T(8,128)(2,1)S(1)} fusion(bf16[16384,128]{1,0:T(8,128)(2,1)} %get-tuple-element.126, s32[4096]{0:T(1024)S(1)} %fusion.24), kind=kCustom, calls=%fused_computation.3.clone | custom fusion | bytes 2113536 | tf_op jit(solution)/shard_map/cond/branch_0_fun/jit(_take)/gather | solution.py:66
  574.7 13.8 %gather_fusion.2 = bf16[4096,128]{1,0:T(8,128)(2,1)S(1)} fusion(bf16[16384,128]{1,0:T(8,128)(2,1)} %get-tuple-element.124, s32[4096]{0:T(1024)S(1)} %fusion.24), kind=kCustom, calls=%fused_computation.clone | custom fusion | bytes 2113536 | tf_op jit(solution)/shard_map/cond/branch_0_fun/jit(_take)/gather | solution.py:66
  588.5 2.2 select_bitcast_fusion.1
  590.6 3.1 maximum_select_fusion
  593.8 0.0 all-gather.6.cloned.1.call-update
  593.8 16.9 %copy.106 = bf16[384,16384]{0,1:T(8,128)(2,1)} copy(bf16[384,16384]{1,0:T(8,128)(2,1)} %get-tuple-element.313) | data formatting | bytes 25165824 | tf_op jit(solution)/shard_map
  610.7 133.0 %gather_fusion.1 = bf16[32768,384]{1,0:T(8,128)(2,1)} fusion(bf16[16384,384]{1,0:T(8,128)(2,1)} %bitcast.122, s32[32768]{0:T(1024)S(1)} %broadcast_clamp_fusion), kind=kCustom, calls=%fused_computation.5 | custom fusion | bytes 50462720 | tf_op jit(solution)/shard_map/cond/branch_0_fun/jit(_take)/gather | solution.py:70
  743.8 0.1 broadcast_compare_fusion
  743.9 78.8 %all-gather.6.cloned.1.call-done = bf16[8,4096,256]{2,1,0:T(8,128)(2,1)} async-done(((bf16[1,4096,256]{2,1,0:T(8,128)(2,1)}), bf16[8,4096,256]{2,1,0:T(8,128)(2,1)}) %all-gather.6.cloned.1.call-update) | async-done | bytes 16777232 | tf_op jit(solution)/shard_map/cond/branch_0_fun/all_gather | solution.py:69
  822.7 19.3 %fusion.11 = f32[8,256,384]{2,1,0:T(8,128)S(1)} fusion(bf16[8,4096,256]{2,1,0:T(8,128)(2,1)} %all-gather.6.cloned.1.call-done, bf16[8,4096,384]{2,1,0:T(8,128)(2,1)} %bitcast.128, pred[8,4096]{1,0:T(8,128)(4,1)S(1)} %compare_and_fusion), kind=kOutput, calls=%fused_computation.32 | convolution fusion | flops 6455033856 | bytes 45121536 | tf_op jit(solution)/shard_map/cond/branch_0_fun/imq,imp->iqp/dot_general | solution.py:71
  841.9 0.2 fusion.15
  859.6 0.0 copy-start.1
  859.6 0.0 reduce-scatter.2.cloned.1.call-start
  859.7 1.1 copy-done.1
  860.8 0.0 reduce-scatter.2.cloned.1.call-update
  860.8 28.2 %reduce-scatter.2.cloned.1.call-done = f32[256,384]{1,0:T(8,128)} async-done(((f32[1024,384]{1,0:T(8,128)}), f32[256,384]{1,0:T(8,128)}) %reduce-scatter.2.cloned.1.call-update) | async-done | bytes 393232 | tf_op jit(solution)/shard_map/reduce_scatter | solution.py:81
  889.0 1.7 convert_element_type.31
  (21 shorter events, 0.4 us)
Async XLA Ops:
  14.2 5.0 copy-start.9
  14.2 11.1 %copy-start = (s32[8]{0:T(128)S(1)}, s32[8]{0:T(128)}, u32[]{:S(2)}) copy-start(s32[8]{0:T(128)} %param.19) | copy-start | bytes 100
  14.2 53.9 %all-to-all-start = ((bf16[64,256,128]{2,0,1:T(8,128)(2,1)}), bf16[64,256,128]{2,0,1:T(8,128)(2,1)}, u32[]{:S(2)}, u32[]{:S(2)}) async-start(bf16[64,256,128]{2,0,1:T(8,128)(2,1)} %copy.101), calls=%async_computation | async-start | bytes 8388608 | tf_op jit(solution)/shard_map/all_to_all | solution.py:23
  73.0 4.7 copy-start.16
  77.7 1.9 copy-start.13
  77.7 2.1 copy-start.10
  77.7 744.9 %all-gather.6.cloned.1.call-start = ((), (), s32[]{:S(2)}) async-start(), calls=%async_computation.2 | async-start | bytes 18874368 | tf_op jit(solution)/shard_map/cond/branch_0_fun/all_gather | solution.py:69
  859.6 1.2 copy-start.1
  859.6 29.3 %reduce-scatter.2.cloned.1.call-start = ((), (), s32[]{:S(2)}) async-start(), calls=%async_computation.7 | async-start | bytes 1966080 | tf_op jit(solution)/shard_map/reduce_scatter | solution.py:81
Sparse Core Ops, SparseCore 0:
  593.9 228.7 all-gather.5
Sparse Core Ops, SparseCore 1:
  862.6 26.3 reduce-scatter.1

commit v2 on v1

--- a/solution.py
+++ b/solution.py
@@ -53,26 +53,26 @@
 
             def compact(cap):
                 def run(_):
-                    masks = cd_label[None, :] == block_label[:, None]
-                    pos = jnp.cumsum(masks.astype(jnp.int32), axis=1) - 1
-                    target = jnp.where(masks, pos, cap)
-                    src = jnp.broadcast_to(jnp.arange(cd_count, dtype=jnp.int32), masks.shape)
-                    lane = jnp.broadcast_to(jnp.arange(n_row, dtype=jnp.int32)[:, None], masks.shape)
-                    idx = jnp.zeros((n_row, cap), jnp.int32).at[lane, target].set(src, mode="drop")
-                    valid = jnp.arange(cap)[None, :] < own_counts[:, None]
-                    own_idx = idx[row_i]
-                    own_valid = valid[row_i][:, None]
-                    sent = jnp.concatenate(
-                        [jnp.take(integrals, own_idx, axis=0), jnp.take(mirrored, own_idx, axis=0)], axis=1
-                    )
+                    n_pb = pair_label.shape[0]
+                    pb = pair_rows // n_pb
+                    own_label = block_label[row_i]
+                    wanted = jnp.concatenate([own_label[None], pair_label.astype(block_label.dtype)])
+                    iota = jnp.arange(cd_count, dtype=jnp.int32)
+                    keys = jnp.where(cd_label[None, :] == wanted[:, None], iota[None, :], iota[None, :] + cd_count)
+                    order = jnp.sort(keys, axis=1)[:, :cap]
+                    order = jnp.where(order >= cd_count, order - cd_count, order)
+                    own_valid = (jnp.arange(cap) < own_counts[row_i])[:, None]
+                    both = jnp.concatenate([integrals, mirrored], axis=1)
+                    sent = jnp.take(both, order[0], axis=0)
                     sent = jnp.where(own_valid, sent, jnp.zeros_like(sent))
                     got = lax.all_gather(sent, "row", axis=0, tiled=False)
-                    amp_rows = jnp.take(amplitudes.T, idx, axis=0)
-                    prod = jnp.einsum("imq,imp->iqp", got, amp_rows, preferred_element_type=jnp.float32)
-                    diff = prod[:, :ab_count] - prod[:, ab_count:]
-                    keep = row_label[None, :] == block_label[:, None]
-                    diff = jnp.where(keep[:, None, :], diff, jnp.zeros_like(diff))
-                    return diff.reshape(n_row * ab_count, pair_rows)
+                    amp_t = amplitudes.T.reshape(cd_count, n_pb, pb)
+                    amp_rows = jnp.stack([jnp.take(amp_t[:, u], order[1 + u], axis=0) for u in range(n_pb)])
+                    prod = jnp.einsum("imq,ump->iuqp", got, amp_rows, preferred_element_type=jnp.float32)
+                    diff = prod[:, :, :ab_count] - prod[:, :, ab_count:]
+                    keep = block_label[:, None] == pair_label[None, :]
+                    diff = jnp.where(keep[:, :, None, None], diff, jnp.zeros_like(diff))
+                    return jnp.transpose(diff, (0, 2, 1, 3)).reshape(n_row * ab_count, pair_rows)
 
                 return run
 

time: 906 us -> 438 us (0.48)
  local copies, waits for them, and re-layouts: 678 us -> 139 us
  waiting for transfers between devices: 146 us -> 220 us
  other arithmetic: 15.1 us -> 25 us
    cond x10 -> x7, local copies, waits for them, and re-layouts: 479 us -> 21.6 us
    gather x3 -> x7, local copies, waits for them, and re-layouts: 161 us -> 61.2 us  [the longest x6 43.8 us: run(): jnp.take(amp_t[:, u], order[1 + u], axis=0)]
    all_gather x1, waiting for transfers between devices: 78.8 us -> 154 us  [run(): got = lax.all_gather(sent, 'row', axis=0, tiled=False)]
    sort x0 -> x2, local copies, waits for them, and re-layouts: none -> 25.8 us  [run(): order = jnp.sort(keys, axis=1)[:, :cap]]
    another operation x4 -> x1, local copies, waits for them, and re-layouts: 17 us -> 0.08 us
    slice x0 -> x2, local copies, waits for them, and re-layouts: none -> 9.18 us  [the longest x1 9.14 us: run(): amp_t[:, u]]
  transfers between devices with their start and end apart: 3 -> 3, of which waited for: 3 -> 3; matrix products, arithmetic and copies ran while one was open for 18% -> 19% of each run, Pallas kernels for 0% -> 0%
where the time goes in v2:
time: 438 us; the launch traced here: 430 us
  waiting for transfers between devices  220 us (50%)
  local copies, waits for them, and re-layouts  139 us (32%)
  other arithmetic  25 us (6%)
  between operations  17.1 us (4%)
  loops' own time  12.8 us (3%)
  matrix products  10.6 us (2%)
  starting transfers between devices  5.27 us (1%)
    all_gather x1, waiting for transfers between devices, run(): got = lax.all_gather(sent, 'row', axis=0, tiled=False)  154 us
    gather x6, local copies, waits for them, and re-layouts, run(): jnp.take(amp_t[:, u], order[1 + u], axis=0)  43.8 us
    all_to_all x1, waiting for transfers between devices, body(): lax.all_to_all(int_cube, 'col', split_axis=1, concat_axis=0, tiled=True)  38.8 us
    reduce_scatter x1, waiting for transfers between devices, body(): summed = lax.psum_scatter(partial, 'col', scatter_dimension=0, tiled=True)  27.6 us
    sort x2, local copies, waits for them, and re-layouts, run(): order = jnp.sort(keys, axis=1)[:, :cap]  25.8 us
    cond x6, local copies, waits for them, and re-layouts  19.9 us
    gather x1, local copies, waits for them, and re-layouts, run(): sent = jnp.take(both, order[0], axis=0)  17.4 us
    another operation x1, loops' own time, body(): partial = lax.switch(tier, branches, None)  12.8 us
  transfers between devices with their start and end apart: 3, of which 3 were waited for; matrix products, arithmetic and copies ran while one was open for 19% of the time, Pallas kernels for 0%

profile of v2, /device:TPU:0, one launch (start us, length us, event | category | flops | bytes accessed | tf_op | source)
XLA Modules:
  0.0 430.0 jit_solution(16706893788737114906)
XLA Ops:
  7.4 6.9 %copy.152 = bf16[64,256,128]{2,0,1:T(8,128)(2,1)} copy(bf16[64,256,128]{2,1,0:T(8,128)(2,1)} %bitcast.200) | data formatting | bytes 8388608 | tf_op jit(solution)/shard_map/reshape | solution.py:22
  14.3 0.0 copy-start.4
  14.3 0.0 copy-start
  14.3 5.0 %all-to-all-start = ((bf16[64,256,128]{2,0,1:T(8,128)(2,1)}), bf16[64,256,128]{2,0,1:T(8,128)(2,1)}, u32[]{:S(2)}, u32[]{:S(2)}) async-start(bf16[64,256,128]{2,0,1:T(8,128)(2,1)} %copy.152), calls=%async_computation | async-start | bytes 8388608 | tf_op jit(solution)/shard_map/all_to_all | solution.py:23
  19.3 0.0 copy-done.4
  19.3 0.1 convert_reduce_fusion
  19.4 0.7 fusion.75
  20.1 4.9 %bitcast_select_fusion.3 = s32[256,8]{0,1:T(8,128)S(1)} fusion(s32[]{:T(128)} %bitcast.76, s32[]{:T(128)} %bitcast.77, s32[]{:T(128)} %bitcast.78, s32[]{:T(128)} %bitcast.79, s32[]{:T(128)} %bitcast.80, s32[]{:T(128)} %bitcast.82, s32[]{:T(128)} %bitcast.81, s32[]{:T(128)} %bitcast.75, s32[256]{0:T(256)S(1)} %copy-done.4), kind=kLoop, calls=%fused_computation.155 | loop fusion | flops 36864 | bytes 9248 | tf_op jit(solution)/shard_map/gather | solution.py:46
  25.0 0.1 reshape.513
  25.1 0.2 reduce_sum.19
  25.3 0.0 copy-done
  25.3 0.6 gather_fusion.15
  26.0 0.6 gather_fusion.16
  26.6 0.6 reduce_max.9
  29.1 0.1 dynamic_slice.34
  29.2 0.1 broadcast_xor_fusion
  29.3 38.8 %all-to-all-done = bf16[64,256,128]{2,0,1:T(8,128)(2,1)} async-done(((bf16[64,256,128]{2,0,1:T(8,128)(2,1)}), bf16[64,256,128]{2,0,1:T(8,128)(2,1)}, u32[]{:S(2)}, u32[]{:S(2)}) %all-to-all-start) | async-done | bytes 4194336 | tf_op jit(solution)/shard_map/all_to_all | solution.py:23
  68.1 4.9 %copy.154 = bf16[4,64,64,128]{3,2,1,0:T(8,128)(2,1)S(1)} copy(bf16[4,64,64,128]{3,1,2,0:T(8,128)(2,1)} %bitcast.90) | data formatting | bytes 8388608 | tf_op jit(solution)/shard_map/all_to_all | solution.py:23
  73.0 0.0 copy-start.5
  73.0 4.7 %copy.155 = bf16[64,256,128]{2,1,0:T(8,128)(2,1)} copy(bf16[64,256,128]{2,0,1:T(8,128)(2,1)S(1)} %bitcast.211) | data formatting | bytes 8388608 | tf_op jit(solution)/shard_map/transpose | solution.py:24
  77.7 0.0 copy-done.5
  77.7 313.5 %conditional.1 = (f32[1024,384]{0,1:T(8,128)S(1)}) conditional(s32[]{:T(128)} %clamp.3, (s32[8]{0:T(128)S(1)}, s32[3]{0:T(128)S(1)}, bf16[384,16384]{1,0:T(8,128)(2,1)}, s32[64,256]{1,0:T(8,128)S(1)}, s32[]{:T(128)}, /*index=5*/s32[]{:T(128)}, s32[4,8]{0,1:T(8,128)S(1)}, s32[8,1]{0,1:T(1,128)S(1)}, ...), branch_computations={%region_3.6_spmd, %region_5.9_spmd, %region_7.12_spmd, %region_9.1... | conditional | flops 25862471680 | bytes 326910592 | solution.py:80
  77.7 0.0 sort.19.cloned.1.call-start
  77.8 0.6 dynamic_slice.24
  78.4 0.6 pad_add_fusion
  79.0 0.9 iota_select_fusion
  79.8 0.0 sort.19.cloned.1.call-update
  79.9 0.3 all-gather.6.cloned.1.call-start
  80.1 7.2 %pad_maximum_fusion = bf16[16384,256]{1,0:T(8,128)(2,1)} fusion(bf16[16384,128]{1,0:T(8,128)(2,1)} %get-tuple-element.127, bf16[16384,128]{1,0:T(8,128)(2,1)} %get-tuple-element.126), kind=kLoop, calls=%fused_computation.35 | loop fusion | flops 16777216 | bytes 16777216 | tf_op jit(solution)/shard_map/cond/branch_0_fun/concatenate | solution.py:65
  87.3 0.1 copy.156
  87.4 0.6 gather_fusion
  88.1 0.6 dynamic_slice.26
  88.7 25.8 %sort.19.cloned.1.call-done = s32[4,16384]{1,0:T(4,128)} async-done(((s32[4,16384]{1,0:T(4,128)}), s32[4,16384]{1,0:T(4,128)}) %sort.19.cloned.1.call-update) | async-done | bytes 262160 | tf_op jit(solution)/shard_map/cond/branch_0_fun/jit(sort)/sort | solution.py:62
  114.5 0.9 compare_select_fusion.11
  115.4 17.4 %gather_fusion.1 = bf16[4096,256]{1,0:T(8,128)(2,1)S(1)} fusion(bf16[16384,256]{1,0:T(8,128)(2,1)} %pad_maximum_fusion, s32[4096]{0:T(1024)S(1)} %broadcast_clamp_fusion), kind=kCustom, calls=%fused_computation.6 | custom fusion | bytes 4210688 | tf_op jit(solution)/shard_map/cond/branch_0_fun/jit(_take)/gather | solution.py:66
  132.9 0.6 iota_compare_fusion
  133.5 4.2 fusion.17
  137.6 0.0 all-gather.6.cloned.1.call-update
  137.6 9.1 %fusion.69 = (bf16[16384,1,128]{0,2,1:T(8,128)(2,1)}, bf16[16384,1,128]{0,2,1:T(8,128)(2,1)}, bf16[16384,1,128]{0,2,1:T(8,128)(2,1)}) fusion(bf16[16384,3,128]{0,2,1:T(8,128)(2,1)} %bitcast.194), kind=kLoop, calls=%fused_computation.176 | loop fusion | bytes 25165824 | tf_op jit(solution)/shard_map/cond/branch_0_fun/slice | solution.py:70
  146.8 6.7 %copy.166 = bf16[16384,1,128]{2,0,1:T(8,128)(2,1)} copy(bf16[16384,1,128]{0,2,1:T(8,128)(2,1)} %get-tuple-element.337) | data formatting | bytes 8388608 | tf_op jit(solution)/shard_map/cond
  153.5 6.4 %copy.165 = bf16[16384,1,128]{2,0,1:T(8,128)(2,1)} copy(bf16[16384,1,128]{0,2,1:T(8,128)(2,1)} %get-tuple-element.336) | data formatting | bytes 8388608 | tf_op jit(solution)/shard_map/cond
  159.9 6.4 %copy.164 = bf16[16384,1,128]{2,0,1:T(8,128)(2,1)} copy(bf16[16384,1,128]{0,2,1:T(8,128)(2,1)} %get-tuple-element.335) | data formatting | bytes 8388608 | tf_op jit(solution)/shard_map/cond
  166.3 0.1 broadcast_compare_fusion
  166.4 13.8 %gather_fusion.4 = bf16[4096,128]{1,0:T(8,128)(2,1)S(1)} fusion(bf16[16384,128]{1,0:T(8,128)(2,1)} %bitcast.210, s32[4096]{0:T(1024)S(1)} %fusion.25), kind=kCustom, calls=%fused_computation.4.clone | custom fusion | bytes 2113536 | tf_op jit(solution)/shard_map/cond/branch_0_fun/jit(_take)/gather | solution.py:70
  180.2 0.5 copy.136
  180.7 13.8 %gather_fusion.3 = bf16[4096,128]{1,0:T(8,128)(2,1)S(1)} fusion(bf16[16384,128]{1,0:T(8,128)(2,1)} %bitcast.209, s32[4096]{0:T(1024)S(1)} %fusion.24), kind=kCustom, calls=%fused_computation.3.clone | custom fusion | bytes 2113536 | tf_op jit(solution)/shard_map/cond/branch_0_fun/jit(_take)/gather | solution.py:70
  194.5 1.3 copy.134
  195.9 13.8 %gather_fusion.2 = bf16[4096,128]{1,0:T(8,128)(2,1)S(1)} fusion(bf16[16384,128]{1,0:T(8,128)(2,1)} %bitcast.208, s32[4096]{0:T(1024)S(1)} %fusion.23), kind=kCustom, calls=%fused_computation.clone | custom fusion | bytes 2113536 | tf_op jit(solution)/shard_map/cond/branch_0_fun/jit(_take)/gather | solution.py:70
  209.7 0.5 copy.132
  210.3 0.1 select_bitcast_fusion.2
  210.4 2.5 select_bitcast_fusion
  212.9 153.6 %all-gather.6.cloned.1.call-done = bf16[8,4096,256]{2,1,0:T(8,128)(2,1)} async-done(((bf16[1,4096,256]{2,1,0:T(8,128)(2,1)}), bf16[8,4096,256]{2,1,0:T(8,128)(2,1)}) %all-gather.6.cloned.1.call-update) | async-done | bytes 16777232 | tf_op jit(solution)/shard_map/cond/branch_0_fun/all_gather | solution.py:68
  366.5 10.6 %fusion.18 = f32[8,3,256,128]{2,3,0,1:T(8,128)S(1)} fusion(bf16[8,4096,256]{2,1,0:T(8,128)(2,1)} %all-gather.6.cloned.1.call-done, bf16[1,4096,128]{1,2,0:T(8,128)(2,1)S(1)} %get-tuple-element.344, bf16[1,4096,128]{1,2,0:T(8,128)(2,1)} %get-tuple-element.345, bf16[1,4096,128]{1,2,0:T(8,128)(2,1)S(1)} %select_bitcast_fusion.2), kind=kOutput, calls=%fused_computation.43 | convolution fusion | flops 6451888128 | bytes 23068672 | tf_op jit(solution)/shard_map/cond/branch_0_fun/imq,ump->iuqp/dot_general | solution.py:71
  377.1 0.3 fusion.22
  377.4 0.9 copy.137
  378.3 0.3 copy.183
  391.2 0.0 reduce-scatter.2.cloned.1.call-start
  391.3 1.7 copy.159
  392.9 0.0 reduce-scatter.2.cloned.1.call-update
  393.0 27.6 %reduce-scatter.2.cloned.1.call-done = f32[256,384]{1,0:T(8,128)} async-done(((f32[1024,384]{1,0:T(8,128)}), f32[256,384]{1,0:T(8,128)}) %reduce-scatter.2.cloned.1.call-update) | async-done | bytes 393232 | tf_op jit(solution)/shard_map/reduce_scatter | solution.py:81
  420.6 1.7 convert_element_type.19
  (17 shorter events, 0.2 us)
Async XLA Ops:
  14.3 5.0 %copy-start.4 = (s32[256]{0:T(256)S(1)}, s32[256]{0:T(256)}, u32[]{:S(2)}) copy-start(s32[256]{0:T(256)} %param.18) | copy-start | bytes 3076
  14.3 11.0 %copy-start = (s32[8]{0:T(128)S(1)}, s32[8]{0:T(128)}, u32[]{:S(2)}) copy-start(s32[8]{0:T(128)} %param.19) | copy-start | bytes 100
  14.3 53.8 %all-to-all-start = ((bf16[64,256,128]{2,0,1:T(8,128)(2,1)}), bf16[64,256,128]{2,0,1:T(8,128)(2,1)}, u32[]{:S(2)}, u32[]{:S(2)}) async-start(bf16[64,256,128]{2,0,1:T(8,128)(2,1)} %copy.152), calls=%async_computation | async-start | bytes 8388608 | tf_op jit(solution)/shard_map/all_to_all | solution.py:23
  73.0 4.7 %copy-start.5 = (s32[3]{0:T(128)S(1)}, s32[3]{0:T(128)}, u32[]{:S(2)}) copy-start(s32[3]{0:T(128)} %param.17) | copy-start | bytes 40
  77.7 36.8 %sort.19.cloned.1.call-start = ((), (), s32[]{:S(2)}) async-start(), calls=%async_computation.8 | async-start | bytes 786464 | tf_op jit(solution)/shard_map/cond/branch_0_fun/jit(sort)/sort | solution.py:62
  79.9 286.6 %all-gather.6.cloned.1.call-start = ((), (), s32[]{:S(2)}) async-start(), calls=%async_computation.2 | async-start | bytes 18874368 | tf_op jit(solution)/shard_map/cond/branch_0_fun/all_gather | solution.py:68
  391.2 29.3 %reduce-scatter.2.cloned.1.call-start = ((), (), s32[]{:S(2)}) async-start(), calls=%async_computation.7 | async-start | bytes 1966080 | tf_op jit(solution)/shard_map/reduce_scatter | solution.py:81
Sparse Core Ops, SparseCore 0:
  81.0 33.2 sort.25.cloned.1.call-done
  137.8 228.7 all-gather.5
  (1 shorter events, 0.0 us)
Sparse Core Ops, SparseCore 1:
  394.2 26.3 reduce-scatter.1

commit v3 on v2

--- a/solution.py
+++ b/solution.py
@@ -19,11 +19,11 @@
         c_irrep = lax.dynamic_slice_in_dim(orbital_irrep, col_i * c_count, c_count)
         cd_label = jnp.bitwise_xor(c_irrep[:, None], orbital_irrep[None, :]).reshape(cd_count)
         row_label = jnp.repeat(pair_label, pair_rows // pair_label.shape[0])
-        int_cube = integrals.reshape(c_count, orb_width, ab_count)
-        swapped = lax.all_to_all(int_cube, "col", split_axis=1, concat_axis=0, tiled=True)
-        mirrored = jnp.transpose(swapped, (1, 0, 2)).reshape(cd_count, ab_count)
 
         def dense(_):
+            int_cube = integrals.reshape(c_count, orb_width, ab_count)
+            swapped = lax.all_to_all(int_cube, "col", split_axis=1, concat_axis=0, tiled=True)
+            mirrored = jnp.transpose(swapped, (1, 0, 2)).reshape(cd_count, ab_count)
             ab_label = jnp.repeat(column_label, PAIR_BLOCK)
             amp_keep = row_label[:, None] == cd_label[None, :]
             slab_keep = cd_label[:, None] == ab_label[None, :]
@@ -55,21 +55,30 @@
                 def run(_):
                     n_pb = pair_label.shape[0]
                     pb = pair_rows // n_pb
-                    own_label = block_label[row_i]
-                    wanted = jnp.concatenate([own_label[None], pair_label.astype(block_label.dtype)])
                     iota = jnp.arange(cd_count, dtype=jnp.int32)
-                    keys = jnp.where(cd_label[None, :] == wanted[:, None], iota[None, :], iota[None, :] + cd_count)
-                    order = jnp.sort(keys, axis=1)[:, :cap]
-                    order = jnp.where(order >= cd_count, order - cd_count, order)
+
+                    def first(masks):
+                        keys = jnp.where(masks, iota[None, :], iota[None, :] + cd_count)
+                        order = jnp.sort(keys, axis=1)[:, :cap]
+                        return jnp.where(order >= cd_count, order - cd_count, order)
+
+                    own_order = first((cd_label == block_label[row_i])[None, :])[0]
                     own_valid = (jnp.arange(cap) < own_counts[row_i])[:, None]
-                    both = jnp.concatenate([integrals, mirrored], axis=1)
-                    sent = jnp.take(both, order[0], axis=0)
+                    sent = jnp.take(integrals, own_order, axis=0)
                     sent = jnp.where(own_valid, sent, jnp.zeros_like(sent))
                     got = lax.all_gather(sent, "row", axis=0, tiled=False)
-                    amp_t = amplitudes.T.reshape(cd_count, n_pb, pb)
-                    amp_rows = jnp.stack([jnp.take(amp_t[:, u], order[1 + u], axis=0) for u in range(n_pb)])
+                    amp_t = amplitudes.T
+                    amp_swap = lax.all_to_all(
+                        amp_t.reshape(c_count, orb_width, pair_rows), "col", split_axis=1, concat_axis=0, tiled=True
+                    )
+                    amp_mirror = jnp.transpose(amp_swap, (1, 0, 2)).reshape(cd_count, pair_rows)
+                    p_order = first(cd_label[None, :] == pair_label[:, None].astype(cd_label.dtype))
+                    both = jnp.concatenate(
+                        [amp_t.reshape(cd_count, n_pb, pb), amp_mirror.reshape(cd_count, n_pb, pb)], axis=2
+                    )
+                    amp_rows = jnp.stack([jnp.take(both[:, u], p_order[u], axis=0) for u in range(n_pb)])
                     prod = jnp.einsum("imq,ump->iuqp", got, amp_rows, preferred_element_type=jnp.float32)
-                    diff = prod[:, :, :ab_count] - prod[:, :, ab_count:]
+                    diff = prod[..., :pb] - prod[..., pb:]
                     keep = block_label[:, None] == pair_label[None, :]
                     diff = jnp.where(keep[:, :, None, None], diff, jnp.zeros_like(diff))
                     return jnp.transpose(diff, (0, 2, 1, 3)).reshape(n_row * ab_count, pair_rows)

time: 438 us -> 498 us (1.14)
  local copies, waits for them, and re-layouts: 139 us -> 241 us
  waiting for transfers between devices: 220 us -> 152 us
  other arithmetic: 25 us -> 41.7 us
  loops' own time: 12.8 us -> 20 us
    all_gather x1, waiting for transfers between devices: 154 us -> 0.01 us  [run(): got = lax.all_gather(sent, 'row', axis=0, tiled=False)]
    all_to_all x1, waiting for transfers between devices: 38.8 us -> 121 us  [run(): lax.all_to_all(amp_t.reshape(c_count, orb_width, pair_rows), 'col', split...]
    reshape x1 -> x4, local copies, waits for them, and re-layouts: 6.91 us -> 71 us  [the longest x2 36.1 us: run(): amp_mirror.reshape(cd_count, n_pb, pb)]
    gather x7, local copies, waits for them, and re-layouts: 61.2 us -> 86 us  [the longest x6 72.3 us: run(): jnp.take(both[:, u], p_order[u], axis=0)]
    squeeze x0 -> x1, other arithmetic: none -> 16.9 us  [run(): both[:, u]]
    transpose x1, local copies, waits for them, and re-layouts: 4.69 us -> 18 us  [run(): amp_mirror = jnp.transpose(amp_swap, (1, 0, 2)).reshape(cd_count, pair_rows)]
    all_to_all x1, local copies, waits for them, and re-layouts: 4.89 us -> 14.5 us  [run(): lax.all_to_all(amp_t.reshape(c_count, orb_width, pair_rows), 'col', split...]
    slice x2 -> x1, local copies, waits for them, and re-layouts: 9.18 us -> 0.04 us  [run(): p_order[u]]
  transfers between devices with their start and end apart: 3 -> 3, of which waited for: 3 -> 2; matrix products, arithmetic and copies ran while one was open for 19% -> 43% of each run, Pallas kernels for 0% -> 0%
where the time goes in v3:
time: 498 us; the launch traced here: 490 us
  local copies, waits for them, and re-layouts  241 us (48%)
  waiting for transfers between devices  152 us (31%)
  other arithmetic  41.7 us (8%)
  loops' own time  20 us (4%)
  between operations  16.7 us (3%)
  matrix products  11.7 us (2%)
  starting transfers between devices  6.74 us (1%)
    all_to_all x1, waiting for transfers between devices, run(): lax.all_to_all(amp_t.reshape(c_count, orb_width, pair_rows), 'col', split...  121 us
    gather x6, local copies, waits for them, and re-layouts, run(): jnp.take(both[:, u], p_order[u], axis=0)  72.3 us
    reshape x2, local copies, waits for them, and re-layouts, run(): amp_mirror.reshape(cd_count, n_pb, pb)  36.1 us
    sort x4, local copies, waits for them, and re-layouts, first(): order = jnp.sort(keys, axis=1)[:, :cap]  30.8 us
    reduce_scatter x1, waiting for transfers between devices, body(): summed = lax.psum_scatter(partial, 'col', scatter_dimension=0, tiled=True)  30.6 us
    another operation x1, loops' own time, body(): partial = lax.switch(tier, branches, None)  20 us
    reshape x1, local copies, waits for them, and re-layouts, run(): amp_t.reshape(c_count, orb_width, pair_rows)  18.3 us
    transpose x1, local copies, waits for them, and re-layouts, run(): amp_mirror = jnp.transpose(amp_swap, (1, 0, 2)).reshape(cd_count, pair_rows)  18 us
  transfers between devices with their start and end apart: 3, of which 2 were waited for; matrix products, arithmetic and copies ran while one was open for 43% of the time, Pallas kernels for 0%

profile of v3, /device:TPU:0, one launch (start us, length us, event | category | flops | bytes accessed | tf_op | source)
XLA Modules:
  0.0 490.0 jit_solution(15582539054870855488)
XLA Ops:
  7.4 0.8 convert_reduce_fusion
  8.2 0.7 fusion.90
  8.8 5.6 %bitcast_select_fusion.3 = s32[256,8]{0,1:T(8,128)S(1)} fusion(s32[]{:T(128)} %bitcast.98, s32[]{:T(128)} %bitcast.99, s32[]{:T(128)} %bitcast.100, s32[]{:T(128)} %bitcast.101, s32[]{:T(128)} %bitcast.102, s32[]{:T(128)} %bitcast.104, s32[]{:T(128)} %bitcast.103, s32[]{:T(128)} %bitcast.97, s32[256]{0:T(256)} %param.18), kind=kLoop, calls=%fused_computation.191 | loop fusion | flops 36864 | bytes 9248 | tf_op jit(solution)/shard_map/gather | solution.py:46
  14.5 0.1 reshape.627
  14.5 0.2 reduce_sum.19
  14.8 0.8 dynamic_slice.34
  15.5 0.8 broadcast_xor_fusion
  16.3 1.3 gather_fusion.15
  17.6 0.6 gather_fusion.16
  18.2 0.6 reduce_max.9
  20.7 0.1 xor.58
  20.8 0.7 xor.59
  21.5 427.1 %conditional.1 = (f32[1024,384]{0,1:T(8,128)S(1)}) conditional(s32[]{:T(128)} %clamp.3, (s32[8]{0:T(128)S(1)}, s32[3]{0:T(128)}, bf16[384,16384]{1,0:T(8,128)(2,1)}, s32[64,256]{1,0:T(8,128)S(1)}, s32[]{:T(128)}, /*index=5*/s32[4,8]{0,1:T(8,128)S(1)}, s32[8,1]{0,1:T(1,128)S(1)}, s32[]{:T(128)}, ...), branch_computations={%region_3.7_spmd, %region_6.11_spmd, %region_9.15_spmd, %region_12... | conditional | flops 25862471680 | bytes 485741536 | solution.py:89
  21.5 0.0 sort.39.cloned.1.call-start
  21.5 0.6 dynamic_slice.26
  22.1 0.7 fusion.28
  22.8 0.1 copy.213
  22.8 0.7 add_select_fusion
  23.6 0.0 sort.39.cloned.1.call-update
  23.6 0.0 sort.37.cloned.1.call-start
  23.7 1.5 iota_select_fusion
  25.2 0.0 sort.37.cloned.1.call-update
  25.2 0.0 all-gather.6.cloned.1.call-start
  25.3 0.1 copy.199
  25.4 0.6 gather_fusion
  26.0 0.6 dynamic_slice.25
  26.6 30.7 %sort.39.cloned.1.call-done = s32[1,16384]{1,0:T(1,128)} async-done(((s32[1,16384]{1,0:T(1,128)}), s32[1,16384]{1,0:T(1,128)}) %sort.39.cloned.1.call-update) | async-done | bytes 65552 | tf_op jit(solution)/shard_map/cond/branch_0_fun/jit(sort)/sort | solution.py:62
  57.3 0.7 compare_select_fusion.12
  58.1 0.6 iota_compare_fusion
  58.7 13.8 %gather_fusion.1 = bf16[4096,128]{1,0:T(8,128)(2,1)S(1)} fusion(bf16[16384,128]{1,0:T(8,128)(2,1)} %get-tuple-element.141, s32[4096]{0:T(1024)S(1)} %broadcast_clamp_fusion), kind=kCustom, calls=%fused_computation.6 | custom fusion | bytes 2113536 | tf_op jit(solution)/shard_map/cond/branch_0_fun/jit(_take)/gather | solution.py:67
  72.4 2.5 fusion.27
  74.9 0.0 all-gather.6.cloned.1.call-update
  74.9 12.0 %copy.212 = bf16[48,8,64,256]{3,2,1,0:T(8,128)(2,1)} copy(bf16[48,8,64,256]{3,1,2,0:T(8,128)(2,1)} %bitcast.255) | data formatting | bytes 25165824 | tf_op jit(solution)/shard_map/cond
  86.9 18.3 %copy.169 = bf16[64,256,384]{2,0,1:T(8,128)(2,1)} copy(bf16[64,256,384]{1,0,2:T(8,128)(2,1)} %bitcast.264) | data formatting | bytes 25165824 | tf_op jit(solution)/shard_map/cond/branch_0_fun/reshape | solution.py:72
  105.2 6.7 %all-to-all-start = ((bf16[64,256,384]{2,0,1:T(8,128)(2,1)}), bf16[64,256,384]{2,0,1:T(8,128)(2,1)}, u32[]{:S(2)}, u32[]{:S(2)}) async-start(bf16[64,256,384]{2,0,1:T(8,128)(2,1)} %copy.169), calls=%async_computation | async-start | bytes 25165824 | tf_op jit(solution)/shard_map/cond/branch_0_fun/all_to_all | solution.py:71
  111.9 0.0 copy-start.4
  111.9 16.6 %copy.173 = bf16[16384,3,128]{2,0,1:T(8,128)(2,1)} copy(bf16[16384,3,128]{0,2,1:T(8,128)(2,1)} %bitcast.256) | data formatting | bytes 25165824 | tf_op jit(solution)/shard_map/cond/branch_0_fun/reshape | solution.py:77
  128.5 0.0 copy-done.4
  128.5 0.1 broadcast_compare_fusion
  128.6 0.9 compare_select_fusion.11
  129.6 121.0 %all-to-all-done = bf16[64,256,384]{2,0,1:T(8,128)(2,1)} async-done(((bf16[64,256,384]{2,0,1:T(8,128)(2,1)}), bf16[64,256,384]{2,0,1:T(8,128)(2,1)}, u32[]{:S(2)}, u32[]{:S(2)}) %all-to-all-start) | async-done | bytes 12582944 | tf_op jit(solution)/shard_map/cond/branch_0_fun/all_to_all | solution.py:71
  250.6 14.5 %copy.171 = bf16[4,64,64,384]{3,2,1,0:T(8,128)(2,1)} copy(bf16[4,64,64,384]{3,1,2,0:T(8,128)(2,1)} %bitcast.5) | data formatting | bytes 25165824 | tf_op jit(solution)/shard_map/cond/branch_0_fun/all_to_all | solution.py:71
  265.1 18.0 %copy.172 = bf16[64,256,384]{1,0,2:T(8,128)(2,1)} copy(bf16[64,256,384]{2,0,1:T(8,128)(2,1)} %bitcast.261) | data formatting | bytes 25165824 | tf_op jit(solution)/shard_map/cond/branch_0_fun/transpose | solution.py:74
  283.1 19.6 %reshape.614 = bf16[16384,3,128]{0,2,1:T(8,128)(2,1)} reshape(bf16[64,256,384]{1,0,2:T(8,128)(2,1)} %copy.172) | data formatting | bytes 25165824 | tf_op jit(solution)/shard_map/cond/branch_0_fun/reshape;cond/branch_0_fun/reshape | solution.py:77
  302.7 16.6 %copy.174 = bf16[16384,3,128]{2,0,1:T(8,128)(2,1)} copy(bf16[16384,3,128]{0,2,1:T(8,128)(2,1)} %reshape.614) | data formatting | bytes 25165824 | tf_op jit(solution)/shard_map/cond/branch_0_fun/reshape;cond/branch_0_fun/reshape | solution.py:77
  319.2 16.9 %fusion.14 = (bf16[16384,256]{1,0:T(8,128)(2,1)}, bf16[16384,256]{1,0:T(8,128)(2,1)}, bf16[16384,256]{1,0:T(8,128)(2,1)}) fusion(bf16[16384,3,128]{2,0,1:T(8,128)(2,1)} %copy.173, bf16[16384,3,128]{2,0,1:T(8,128)(2,1)} %copy.174), kind=kLoop, calls=%fused_computation.40 | loop fusion | flops 50331648 | bytes 50331648 | tf_op jit(solution)/shard_map/cond/branch_0_fun/squeeze | solution.py:79
  336.1 20.4 %gather_fusion.3 = bf16[4096,256]{1,0:T(8,128)(2,1)} fusion(bf16[16384,256]{1,0:T(8,128)(2,1)} %get-tuple-element.376, s32[4096]{0:T(1024)S(1)} %fusion.30), kind=kCustom, calls=%fused_computation.3.clone | custom fusion | bytes 4210688 | tf_op jit(solution)/shard_map/cond/branch_0_fun/jit(_take)/gather | solution.py:79
  356.5 2.9 copy.176
  359.4 20.4 %gather_fusion.4 = bf16[4096,256]{1,0:T(8,128)(2,1)} fusion(bf16[16384,256]{1,0:T(8,128)(2,1)} %get-tuple-element.375, s32[4096]{0:T(1024)S(1)} %fusion.31), kind=kCustom, calls=%fused_computation.4.clone | custom fusion | bytes 4210688 | tf_op jit(solution)/shard_map/cond/branch_0_fun/jit(_take)/gather | solution.py:79
  379.8 4.1 copy.177
  383.9 20.4 %gather_fusion.2 = bf16[4096,256]{1,0:T(8,128)(2,1)} fusion(bf16[16384,256]{1,0:T(8,128)(2,1)} %get-tuple-element.374, s32[4096]{0:T(1024)S(1)} %fusion.29), kind=kCustom, calls=%fused_computation.clone | custom fusion | bytes 4210688 | tf_op jit(solution)/shard_map/cond/branch_0_fun/jit(_take)/gather | solution.py:79
  404.3 4.1 copy.175
  408.4 3.1 select_bitcast_fusion.2
  411.5 4.1 select_bitcast_fusion
  415.6 0.0 all-gather.6.cloned.1.call-done
  415.6 11.7 %fusion.22 = f32[8,3,128,256]{2,3,0,1:T(8,128)S(1)} fusion(bf16[8,4096,128]{2,1,0:T(8,128)(2,1)} %all-gather.6.cloned.1.call-done, bf16[1,4096,256]{1,2,0:T(8,128)(2,1)} %get-tuple-element.382, bf16[1,4096,256]{1,2,0:T(8,128)(2,1)} %get-tuple-element.383, bf16[1,4096,256]{1,2,0:T(8,128)(2,1)} %select_bitcast_fusion.2), kind=kOutput, calls=%fused_computation.53 | convolution fusion | flops 6461325312 | bytes 17825792 | tf_op jit(solution)/shard_map/cond/branch_0_fun/imq,ump->iuqp/dot_general | solution.py:80
  427.3 0.3 fusion.26
  427.6 0.9 copy.178
  428.5 0.3 copy.226
  448.6 0.0 reduce-scatter.2.cloned.1.call-start
  448.7 1.7 copy.202
  450.3 0.0 reduce-scatter.2.cloned.1.call-update
  450.4 30.6 %reduce-scatter.2.cloned.1.call-done = f32[256,384]{1,0:T(8,128)} async-done(((f32[1024,384]{1,0:T(8,128)}), f32[256,384]{1,0:T(8,128)}) %reduce-scatter.2.cloned.1.call-update) | async-done | bytes 393232 | tf_op jit(solution)/shard_map/reduce_scatter | solution.py:90
  481.0 1.7 convert_element_type.19
  (17 shorter events, 0.2 us)
Async XLA Ops:
  21.5 35.8 %sort.39.cloned.1.call-start = ((), (), s32[]{:S(2)}) async-start(), calls=%async_computation.12 | async-start | bytes 196640 | tf_op jit(solution)/shard_map/cond/branch_0_fun/jit(sort)/sort | solution.py:62
  23.6 105.0 %sort.37.cloned.1.call-start = ((), (), s32[]{:S(2)}) async-start(), calls=%async_computation.11 | async-start | bytes 786464 | tf_op jit(solution)/shard_map/cond/branch_0_fun/jit(sort)/sort | solution.py:62
  25.2 390.4 %all-gather.6.cloned.1.call-start = ((), (), s32[]{:S(2)}) async-start(), calls=%async_computation.5 | async-start | bytes 9437184 | tf_op jit(solution)/shard_map/cond/branch_0_fun/all_gather | solution.py:69
  105.2 145.3 %all-to-all-start = ((bf16[64,256,384]{2,0,1:T(8,128)(2,1)}), bf16[64,256,384]{2,0,1:T(8,128)(2,1)}, u32[]{:S(2)}, u32[]{:S(2)}) async-start(bf16[64,256,384]{2,0,1:T(8,128)(2,1)} %copy.169), calls=%async_computation | async-start | bytes 25165824 | tf_op jit(solution)/shard_map/cond/branch_0_fun/all_to_all | solution.py:71
  111.9 16.6 %copy-start.4 = (s32[3]{0:T(128)S(1)}, s32[3]{0:T(128)}, u32[]{:S(2)}) copy-start(s32[3]{0:T(128)} %get-tuple-element.132) | copy-start | bytes 40 | tf_op jit(solution)/shard_map/cond
  448.6 32.4 %reduce-scatter.2.cloned.1.call-start = ((), (), s32[]{:S(2)}) async-start(), calls=%async_computation.10 | async-start | bytes 1966080 | tf_op jit(solution)/shard_map/reduce_scatter | solution.py:90
Sparse Core Ops, SparseCore 0:
  24.8 32.2 sort.51.cloned.1.call-done
  59.9 32.3 sort.49.cloned.1.call-done
  94.9 127.6 all-gather.5
  (2 shorter events, 0.0 us)
Sparse Core Ops, SparseCore 1:
  451.8 29.1 reduce-scatter.1

commit v4 on v3

--- a/solution.py
+++ b/solution.py
@@ -67,16 +67,26 @@
                     sent = jnp.take(integrals, own_order, axis=0)
                     sent = jnp.where(own_valid, sent, jnp.zeros_like(sent))
                     got = lax.all_gather(sent, "row", axis=0, tiled=False)
-                    amp_t = amplitudes.T
-                    amp_swap = lax.all_to_all(
-                        amp_t.reshape(c_count, orb_width, pair_rows), "col", split_axis=1, concat_axis=0, tiled=True
+                    amp_dc = jnp.transpose(amplitudes.reshape(pair_rows, c_count, orb_width), (2, 1, 0))
+                    amp_dc = amp_dc.reshape(cd_count, pair_rows)
+                    received = lax.all_to_all(amp_dc, "col", split_axis=0, concat_axis=0, tiled=True)
+                    p_order = first(cd_label[None, :] == pair_label[:, None].astype(cd_label.dtype))
+                    c_loc = p_order // orb_width
+                    d_all = p_order % orb_width
+                    direct_at = d_all * c_count + c_loc
+                    mirror_at = ((d_all // c_count) * c_count + c_loc) * c_count + d_all % c_count
+                    amp_rows = jnp.stack(
+                        [
+                            jnp.concatenate(
+                                [
+                                    jnp.take(amp_dc[:, u * pb:(u + 1) * pb], direct_at[u], axis=0),
+                                    jnp.take(received[:, u * pb:(u + 1) * pb], mirror_at[u], axis=0),
+                                ],
+                                axis=1,
+                            )
+                            for u in range(n_pb)
+                        ]
                     )
-                    amp_mirror = jnp.transpose(amp_swap, (1, 0, 2)).reshape(cd_count, pair_rows)
-                    p_order = first(cd_label[None, :] == pair_label[:, None].astype(cd_label.dtype))
-                    both = jnp.concatenate(
-                        [amp_t.reshape(cd_count, n_pb, pb), amp_mirror.reshape(cd_count, n_pb, pb)], axis=2
-                    )
-                    amp_rows = jnp.stack([jnp.take(both[:, u], p_order[u], axis=0) for u in range(n_pb)])
                     prod = jnp.einsum("imq,ump->iuqp", got, amp_rows, preferred_element_type=jnp.float32)
                     diff = prod[..., :pb] - prod[..., pb:]
                     keep = block_label[:, None] == pair_label[None, :]

time: 498 us -> 339 us (0.68)
  local copies, waits for them, and re-layouts: 241 us -> 168 us
  waiting for transfers between devices: 152 us -> 84.4 us
  other arithmetic: 41.7 us -> 27.1 us
    all_to_all x1, waiting for transfers between devices: 121 us -> 53.7 us  [run(): lax.all_to_all(amp_dc, 'col', split_axis=0, concat_axis=0, tiled=True)]
    reshape x4 -> x1, local copies, waits for them, and re-layouts: 71 us -> 18.3 us  [run(): amplitudes.reshape(pair_rows, c_count, orb_width)]
    sort x4, local copies, waits for them, and re-layouts: 30.8 us -> 7.43 us  [first(): order = jnp.sort(keys, axis=1)[:, :cap]]
    slice x1 -> x3, local copies, waits for them, and re-layouts: 0.04 us -> 18.9 us  [the longest x1 9.75 us: run(): received[:, u * pb:(u + 1) * pb]]
    transpose x1 -> x0, local copies, waits for them, and re-layouts: 18 us -> none  [run(): amp_mirror = jnp.transpose(amp_swap, (1, 0, 2)).reshape(cd_count, pair_rows)]
    squeeze x1 -> x0, other arithmetic: 16.9 us -> none  [run(): both[:, u]]
    gather x6 -> x12, local copies, waits for them, and re-layouts: 72.3 us -> 87.6 us  [the longest x6 43.9 us: run(): jnp.take(received[:, u * pb:(u + 1) * pb], mirror_at[u], axis=0)]
    all_to_all x1 -> x0, local copies, waits for them, and re-layouts: 14.5 us -> none  [run(): lax.all_to_all(amp_t.reshape(c_count, orb_width, pair_rows), 'col', split...]
  transfers between devices with their start and end apart: 3 -> 3, of which waited for: 2 -> 2; matrix products, arithmetic and copies ran while one was open for 43% -> 41% of each run, Pallas kernels for 0% -> 0%
where the time goes in v4:
time: 339 us; the launch traced here: 335 us
  local copies, waits for them, and re-layouts  168 us (50%)
  waiting for transfers between devices  84.4 us (25%)
  other arithmetic  27.1 us (8%)
  loops' own time  20.4 us (6%)
  between operations  16.7 us (5%)
  matrix products  11.3 us (3%)
  starting transfers between devices  6.7 us (2%)
    all_to_all x1, waiting for transfers between devices, run(): lax.all_to_all(amp_dc, 'col', split_axis=0, concat_axis=0, tiled=True)  53.7 us
    gather x6, local copies, waits for them, and re-layouts, run(): jnp.take(received[:, u * pb:(u + 1) * pb], mirror_at[u], axis=0)  43.9 us
    gather x6, local copies, waits for them, and re-layouts, run(): jnp.take(amp_dc[:, u * pb:(u + 1) * pb], direct_at[u], axis=0)  43.7 us
    reduce_scatter x1, waiting for transfers between devices, body(): summed = lax.psum_scatter(partial, 'col', scatter_dimension=0, tiled=True)  30.7 us
    another operation x1, loops' own time, body(): partial = lax.switch(tier, branches, None)  20.4 us
    reshape x1, local copies, waits for them, and re-layouts, run(): amplitudes.reshape(pair_rows, c_count, orb_width)  18.3 us
    gather x1, local copies, waits for them, and re-layouts, run(): sent = jnp.take(integrals, own_order, axis=0)  13.8 us
    cond x18, local copies, waits for them, and re-layouts  13.4 us
  transfers between devices with their start and end apart: 3, of which 2 were waited for; matrix products, arithmetic and copies ran while one was open for 41% of the time, Pallas kernels for 0%

profile of v4, /device:TPU:0, one launch (start us, length us, event | category | flops | bytes accessed | tf_op | source)
XLA Modules:
  0.0 334.7 jit_solution(18407835268489703578)
XLA Ops:
  7.4 0.8 convert_reduce_fusion
  8.2 0.7 fusion.105
  8.9 5.8 %bitcast_select_fusion = s32[256,8]{0,1:T(8,128)S(1)} fusion(s32[]{:T(128)} %bitcast.86, s32[]{:T(128)} %bitcast.87, s32[]{:T(128)} %bitcast.88, s32[]{:T(128)} %bitcast.89, s32[]{:T(128)} %bitcast.90, s32[]{:T(128)} %bitcast.92, s32[]{:T(128)} %bitcast.91, s32[]{:T(128)} %bitcast.85, s32[256]{0:T(256)} %param.18), kind=kLoop, calls=%fused_computation.269 | loop fusion | flops 36864 | bytes 9248 | tf_op jit(solution)/shard_map/gather | solution.py:46
  14.6 0.1 reshape.390
  14.7 1.3 gather_fusion.24
  16.0 0.2 reduce_sum.19
  16.2 0.6 gather_fusion.25
  16.8 0.6 reduce_max.9
  19.4 0.8 dynamic_slice.34
  20.1 0.8 broadcast_xor_fusion
  20.9 0.1 xor.58
  21.0 0.7 xor.59
  21.7 271.6 %conditional.1 = (f32[1024,384]{0,1:T(8,128)S(1)}) conditional(s32[]{:T(128)} %clamp.3, (s32[8]{0:T(128)S(1)}, s32[3]{0:T(128)}, bf16[384,16384]{1,0:T(8,128)(2,1)}, s32[64,256]{1,0:T(8,128)S(1)}, s32[]{:T(128)}, /*index=5*/s32[4,8]{0,1:T(8,128)S(1)}, s32[8,1]{0,1:T(1,128)S(1)}, s32[]{:T(128)}, ...), branch_computations={%region_3.7_spmd, %region_6.11_spmd, %region_9.15_spmd, %region_12... | conditional | flops 25862471680 | bytes 410948736 | solution.py:99
  21.7 0.6 dynamic_slice.26
  22.2 0.7 fusion.25
  23.0 0.7 add_select_fusion.4
  23.7 12.0 %copy.194 = bf16[48,8,64,256]{3,2,1,0:T(8,128)(2,1)} copy(bf16[48,8,64,256]{3,1,2,0:T(8,128)(2,1)} %bitcast.201) | data formatting | bytes 25165824 | tf_op jit(solution)/shard_map/cond
  35.8 18.3 %copy.160 = bf16[384,64,256]{0,1,2:T(8,128)(2,1)} copy(bf16[384,64,256]{2,1,0:T(8,128)(2,1)} %bitcast.210) | data formatting | bytes 25165824 | tf_op jit(solution)/shard_map/cond/branch_0_fun/reshape | solution.py:70
  54.1 6.4 %all-to-all-start = ((bf16[4,4096,384]{2,1,0:T(8,128)(2,1)}), bf16[4,4096,384]{2,1,0:T(8,128)(2,1)}, u32[]{:S(2)}, u32[]{:S(2)}) async-start(bf16[4,4096,384]{2,1,0:T(8,128)(2,1)} %bitcast.204), calls=%async_computation | async-start | bytes 25165824 | tf_op jit(solution)/shard_map/cond/branch_0_fun/all_to_all | solution.py:72
  60.6 0.9 iota_select_fusion
  61.5 0.2 all-gather.9.cloned.1.call-start
  61.7 0.1 broadcast_compare_fusion.1
  61.8 0.1 copy.184
  61.9 0.6 gather_fusion
  62.6 0.6 dynamic_slice.25
  63.2 9.1 %fusion.93 = (bf16[16384,128]{1,0:T(8,128)(2,1)}, bf16[16384,128]{1,0:T(8,128)(2,1)}, bf16[16384,128]{1,0:T(8,128)(2,1)}) fusion(bf16[16384,384]{1,0:T(8,128)(2,1)} %bitcast.205), kind=kLoop, calls=%fused_computation.290 | loop fusion | bytes 25165824 | tf_op jit(solution)/shard_map/cond/branch_0_fun/slice | solution.py:82
  72.3 0.7 compare_select_fusion.12
  73.0 13.8 %gather_fusion.7 = bf16[4096,128]{1,0:T(8,128)(2,1)S(1)} fusion(bf16[16384,128]{1,0:T(8,128)(2,1)} %get-tuple-element.139, s32[4096]{0:T(1024)S(1)} %fusion.33), kind=kCustom, calls=%fused_computation.8.clone | custom fusion | bytes 2113536 | tf_op jit(solution)/shard_map/cond/branch_0_fun/jit(_take)/gather | solution.py:67
  86.8 0.6 iota_compare_fusion
  87.5 2.5 select_select_fusion
  89.9 7.4 %sort.37.cloned.1.call-done = s32[3,16384]{1,0:T(4,128)} async-done(((s32[3,16384]{1,0:T(4,128)}), s32[3,16384]{1,0:T(4,128)}) %sort.37.cloned.1.call-update) | async-done | bytes 196624 | tf_op jit(solution)/shard_map/cond/branch_0_fun/jit(sort)/sort | solution.py:62
  97.3 1.1 multiply_add_fusion
  98.5 13.7 %gather_fusion.5 = bf16[4096,128]{1,0:T(8,128)(2,1)S(1)} fusion(bf16[16384,128]{1,0:T(8,128)(2,1)} %get-tuple-element.369, s32[4096]{0:T(1024)S(1)} %fusion.31), kind=kCustom, calls=%fused_computation.6.clone | custom fusion | bytes 2113536 | tf_op jit(solution)/shard_map/cond/branch_0_fun/jit(_take)/gather | solution.py:82
  112.3 0.5 copy.165
  112.8 13.8 %gather_fusion.3 = bf16[4096,128]{1,0:T(8,128)(2,1)S(1)} fusion(bf16[16384,128]{1,0:T(8,128)(2,1)} %get-tuple-element.370, s32[4096]{0:T(1024)S(1)} %fusion.29), kind=kCustom, calls=%fused_computation.4.clone | custom fusion | bytes 2113536 | tf_op jit(solution)/shard_map/cond/branch_0_fun/jit(_take)/gather | solution.py:82
  126.6 0.5 copy.163
  127.2 13.8 %gather_fusion.1 = bf16[4096,128]{1,0:T(8,128)(2,1)S(1)} fusion(bf16[16384,128]{1,0:T(8,128)(2,1)} %get-tuple-element.368, s32[4096]{0:T(1024)S(1)} %fusion.27), kind=kCustom, calls=%fused_computation.clone | custom fusion | bytes 2113536 | tf_op jit(solution)/shard_map/cond/branch_0_fun/jit(_take)/gather | solution.py:82
  140.9 1.4 copy.161
  142.4 1.1 broadcast_select_fusion.1
  143.5 1.1 broadcast_select_fusion.3
  144.6 1.1 broadcast_select_fusion.5
  145.7 53.7 %all-to-all-done = bf16[4,4096,384]{2,1,0:T(8,128)(2,1)} async-done(((bf16[4,4096,384]{2,1,0:T(8,128)(2,1)}), bf16[4,4096,384]{2,1,0:T(8,128)(2,1)}, u32[]{:S(2)}, u32[]{:S(2)}) %all-to-all-start) | async-done | bytes 12582944 | tf_op jit(solution)/shard_map/cond/branch_0_fun/all_to_all | solution.py:72
  199.4 9.7 %fusion.94 = (bf16[16384,128]{1,0:T(8,128)(2,1)}, bf16[16384,128]{1,0:T(8,128)(2,1)}, bf16[16384,128]{1,0:T(8,128)(2,1)}) fusion(bf16[16384,384]{1,0:T(8,128)(2,1)} %bitcast.5), kind=kLoop, calls=%fused_computation.291 | loop fusion | bytes 25165824 | tf_op jit(solution)/shard_map/cond/branch_0_fun/slice | solution.py:83
  209.1 13.8 %gather_fusion.6 = bf16[4096,128]{1,0:T(8,128)(2,1)S(1)} fusion(bf16[16384,128]{1,0:T(8,128)(2,1)} %get-tuple-element.372, s32[4096]{0:T(1024)S(1)} %fusion.32), kind=kCustom, calls=%fused_computation.7.clone | custom fusion | bytes 2113536 | tf_op jit(solution)/shard_map/cond/branch_0_fun/jit(_take)/gather | solution.py:83
  222.9 1.4 copy.166
  224.2 13.8 %gather_fusion.4 = bf16[4096,128]{1,0:T(8,128)(2,1)S(1)} fusion(bf16[16384,128]{1,0:T(8,128)(2,1)} %get-tuple-element.373, s32[4096]{0:T(1024)S(1)} %fusion.30), kind=kCustom, calls=%fused_computation.5.clone | custom fusion | bytes 2113536 | tf_op jit(solution)/shard_map/cond/branch_0_fun/jit(_take)/gather | solution.py:83
  238.0 0.5 copy.164
  238.5 13.8 %gather_fusion.2 = bf16[4096,128]{1,0:T(8,128)(2,1)S(1)} fusion(bf16[16384,128]{1,0:T(8,128)(2,1)} %get-tuple-element.371, s32[4096]{0:T(1024)S(1)} %fusion.28), kind=kCustom, calls=%fused_computation.3.clone | custom fusion | bytes 2113536 | tf_op jit(solution)/shard_map/cond/branch_0_fun/jit(_take)/gather | solution.py:83
  252.3 0.7 copy.162
  253.1 1.4 broadcast_select_fusion
  254.5 0.1 copy-done.16
  254.6 1.6 maximum_bitcast_fusion.4
  256.2 0.1 broadcast_select_fusion.2
  256.3 1.6 maximum_bitcast_fusion.3
  257.9 0.1 broadcast_select_fusion.4
  258.0 1.6 maximum_bitcast_fusion.2
  259.6 0.8 copy-done.17
  260.4 11.3 %fusion.16 = f32[8,3,128,256]{2,3,0,1:T(8,128)S(1)} fusion(bf16[8,4096,128,1]{2,1,0,3:T(8,128)(2,1)} %bitcast.281, bf16[1,4096,256]{1,2,0:T(8,128)(2,1)S(1)} %copy-done.17, bf16[1,4096,256]{1,2,0:T(8,128)(2,1)} %maximum_bitcast_fusion.3, bf16[1,4096,256]{1,2,0:T(8,128)(2,1)} %maximum_bitcast_fusion.2), kind=kOutput, calls=%fused_computation.51 | convolution fusion | flops 6461325312 | bytes 17825792 | tf_op jit(solution)/shard_map/cond/branch_0_fun/imq,ump->iuqp/dot_general | solution.py:90
  271.7 0.3 fusion.18
  271.9 0.9 copy.167
  272.8 0.3 copy.208
  293.3 1.6 copy.187
  295.0 30.7 %reduce-scatter.2.cloned.1.call-done = f32[256,384]{1,0:T(8,128)} async-done(((f32[1024,384]{1,0:T(8,128)}), f32[256,384]{1,0:T(8,128)}) %reduce-scatter.2.cloned.1.call-update) | async-done | bytes 393232 | tf_op jit(solution)/shard_map/reduce_scatter | solution.py:100
  325.6 1.7 convert_element_type.19
  (42 shorter events, 0.5 us)
Async XLA Ops:
  21.7 50.6 %sort.39.cloned.1.call-start = ((), (), s32[]{:S(2)}) async-start(), calls=%async_computation.12 | async-start | bytes 196640 | tf_op jit(solution)/shard_map/cond/branch_0_fun/jit(sort)/sort | solution.py:62
  54.1 6.6 %copy-start.18 = (s32[3]{0:T(128)S(1)}, s32[3]{0:T(128)}, u32[]{:S(2)}) copy-start(s32[3]{0:T(128)} %get-tuple-element.132) | copy-start | bytes 40 | tf_op jit(solution)/shard_map/cond
  54.1 145.3 %all-to-all-start = ((bf16[4,4096,384]{2,1,0:T(8,128)(2,1)}), bf16[4,4096,384]{2,1,0:T(8,128)(2,1)}, u32[]{:S(2)}, u32[]{:S(2)}) async-start(bf16[4,4096,384]{2,1,0:T(8,128)(2,1)} %bitcast.204), calls=%async_computation | async-start | bytes 25165824 | tf_op jit(solution)/shard_map/cond/branch_0_fun/all_to_all | solution.py:72
  60.5 36.8 %sort.37.cloned.1.call-start = ((), (), s32[]{:S(2)}) async-start(), calls=%async_computation.11 | async-start | bytes 786464 | tf_op jit(solution)/shard_map/cond/branch_0_fun/jit(sort)/sort | solution.py:62
  61.5 198.1 %all-gather.9.cloned.1.call-start = ((), (), s32[]{:S(2)}) async-start(), calls=%async_computation.5 | async-start | bytes 9437184 | tf_op jit(solution)/shard_map/cond/branch_0_fun/all_gather | solution.py:69
  142.3 2.3 copy-start.13
  253.1 1.5 copy-start.16
  254.6 1.7 copy-start.15
  256.3 1.7 copy-start.14
  258.0 2.3 copy-start.17
  293.3 32.4 %reduce-scatter.2.cloned.1.call-start = ((), (), s32[]{:S(2)}) async-start(), calls=%async_computation.10 | async-start | bytes 1966080 | tf_op jit(solution)/shard_map/reduce_scatter | solution.py:100
Sparse Core Ops, SparseCore 0:
  24.9 33.3 sort.51.cloned.1.call-done
  63.9 33.1 sort.49.cloned.1.call-done
  99.7 128.0 all-gather.8
  (2 shorter events, 0.0 us)
Sparse Core Ops, SparseCore 1:
  296.4 29.1 reduce-scatter.1
